TPU v7x, 256 devices: a whole 4x4x8 slice. The times are simulated.
256 devices in a mesh: sec: 2 (over y_lo), dp: 8 (over x, y_hi), seq: 16 (over z, core).
Axes of the slice: x: 4, y: 4 (y_hi: 2, y_lo: 2; y = y_hi * 2 + y_lo), z: 8, core: 2. Of those that a mesh axis runs over, the one named last changes fastest.
Arguments:
- hidden: bfloat16 [256, 128, 2560], P(('sec', 'dp', 'seq')), may hold values from -24 to 24
- cond_shift: bfloat16 [256, 2560], P(('sec', 'dp', 'seq')), may hold values from -0.3125 to 0.3125
- cond_scale: bfloat16 [256, 2560], P(('sec', 'dp', 'seq')), may hold values from -1.75 to 1.75
- noisy: bfloat16 [256, 128, 256], P(('sec', 'dp', 'seq')), may hold values from -6 to 6
- noise_level: float32 [256], P(('sec', 'dp', 'seq')), may hold values from 0.2 to 1
- w_out: bfloat16 [2560, 256], replicated, may hold values from -0.125 to 0.125
- w_embed: bfloat16 [256, 2048], replicated, may hold values from -0.375 to 0.375
- w_root: bfloat16 [2, 2048], replicated, may hold values from -0.03125 to 0.03125
- w_qkv: bfloat16 [3, 2048, 2048], P(None, None, 'seq'), may hold values from -0.125 to 0.125
- w_proj: bfloat16 [2048, 512], P('seq'), may hold values from -0.125 to 0.125
- text_table: bfloat16 [49408, 512], P('seq'), may hold values from -6 to 6
- text_ids: int32 [32, 32], replicated, may hold values from 0 to 49407
- prompt_index: int32 [256], P(('sec', 'dp')), may hold values from 0 to 31
- reward_weight: float32 [256], P(('sec', 'dp')), may hold values from 1000 to 4000
Outputs:
- rewards: float32 [256], P(('sec', 'dp'))
- grad_w_out: float32 [2560, 256], P('seq')
- grad_hidden: bfloat16 [256, 128, 2560], P(('sec', 'dp', 'seq'))
All inputs are finite; a program needn't handle non-finite values.
Results may differ from a plain program's by a relative error of at most 0.017.
The roundings to bfloat16 on the way count: a program that leaves them out, or rounds other values in their place, can miss the bound.
Values may be sent and summed in bfloat16 or wider, within the bound.
No kernel may reach another device: no remote copies, remote signals or barrier semaphores. Data moves between devices by JAX's collectives and lax.ppermute only.
A program may use at most 128 MiB of HBM per device.

v0:
```python
import jax
import jax.numpy as jnp
from jax import lax
from jax.sharding import PartitionSpec as P

D_REW = 2048
HEADS = 16
PROMPTS = 32
normalizing_sharpness = 10.0
epsilon = 1e-06
highest = lax.Precision.HIGHEST


def rotate(angle, first, second):
    cosine = jnp.cos(angle)
    sine_term = jnp.sin(angle)
    return (cosine * first + sine_term * second, cosine * second - sine_term * first)


def suffix(values):
    return jnp.sum(values, axis=1, keepdims=True) - jnp.cumsum(values, axis=1)


def local_path(motion):
    spin = motion[..., 0]
    theta = jnp.cumsum(spin, axis=1) - spin
    step_east, step_north = rotate(theta, motion[..., 1], motion[..., 2])
    path_east = jnp.cumsum(step_east, axis=1) - step_east
    path_north = jnp.cumsum(step_north, axis=1) - step_north
    return (theta, path_east, path_north)


def embed(motion, root_east, root_north, w_embed, root_rows):
    emb = jnp.einsum(
        "cfe,ed->cfd", motion.astype(jnp.bfloat16), w_embed, preferred_element_type=jnp.float32
    )
    emb = emb + root_east[..., None] * root_rows[0] + root_north[..., None] * root_rows[1]
    scale_rms = jnp.sqrt(jnp.mean(emb * emb, axis=-1, keepdims=True) + epsilon)
    return (emb / scale_rms, scale_rms)


def unit_rows(vectors):
    length = jnp.sqrt(jnp.sum(vectors * vectors, axis=-1, keepdims=True) + epsilon)
    return (vectors / length, length)


def norm_grad(grad, normed, scale_rms):
    return (grad - normed * jnp.mean(grad * normed, axis=-1, keepdims=True)) / scale_rms


def motion_grad(d_emb, normed_e, scale_rms, motion, theta, embed_rows, root_rows):
    d_unemb = norm_grad(d_emb, normed_e, scale_rms)
    d_embedded = jnp.einsum("cfd,ed->cfe", d_unemb, embed_rows, precision=highest)
    grad_east = suffix(jnp.sum(d_unemb * root_rows[0], axis=-1))
    grad_north = suffix(jnp.sum(d_unemb * root_rows[1], axis=-1))
    vel_east = motion[..., 1]
    vel_north = motion[..., 2]
    d_east, d_north = rotate(-theta, grad_east, grad_north)
    cosine = jnp.cos(theta)
    sine_term = jnp.sin(theta)
    d_theta = grad_east * (cosine * vel_north - sine_term * vel_east) - grad_north * (
        cosine * vel_east + sine_term * vel_north
    )
    d_spin = suffix(d_theta)
    return d_embedded.at[..., 0].add(d_spin).at[..., 1].add(d_east).at[..., 2].add(d_north)


def local(
    hidden,
    cond_shift,
    cond_scale,
    noisy,
    noise_level,
    w_out,
    w_embed,
    w_root,
    w_qkv,
    w_proj,
    text_table,
    text_ids,
    prompt_index,
    reward_weight,
):
    clips_dev = hidden.shape[0]
    ways = lax.axis_size("seq")
    me = lax.axis_index("seq")
    head_size = D_REW // HEADS
    root_rows = w_root.astype(jnp.float32)
    embed_rows = w_embed.astype(jnp.float32)
    vocab_rows = text_table.shape[0]
    local_ids = text_ids - me * vocab_rows
    inside = (local_ids >= 0) & (local_ids < vocab_rows)
    picked = jnp.take(text_table, jnp.clip(local_ids, 0, vocab_rows - 1), axis=0).astype(
        jnp.float32
    )
    text_part = jnp.sum(jnp.where(inside[..., None], picked, 0.0), axis=1)
    proj_dev = w_proj.shape[0]
    proj_text = lax.all_gather(
        jnp.concatenate([w_proj.astype(jnp.float32), text_part], axis=0), "seq", axis=0
    )
    proj_rows = proj_text[:, :proj_dev].reshape(ways * proj_dev, w_proj.shape[1])
    text_raw = jnp.sum(proj_text[:, proj_dev:], axis=0)
    text_unit, text_len = unit_rows(text_raw)
    w_all = lax.all_gather(w_qkv, "seq", axis=0)
    hidden_f = hidden.astype(jnp.float32)
    centred = hidden_f - jnp.mean(hidden_f, axis=-1, keepdims=True)
    inv_std = lax.rsqrt(jnp.mean(centred * centred, axis=-1, keepdims=True) + epsilon)
    normed_h = centred * inv_std
    gain = 1.0 + cond_scale.astype(jnp.float32)[:, None, :]
    modulated = (normed_h * gain + cond_shift.astype(jnp.float32)[:, None, :]).astype(jnp.bfloat16)
    eps_pred = jnp.einsum("cfd,de->cfe", modulated, w_out, preferred_element_type=jnp.float32)
    level = noise_level[:, None, None]
    x_clean = noisy.astype(jnp.float32) - level * eps_pred
    theta, path_east, path_north = local_path(x_clean)
    normed_e, scale_rms = embed(x_clean, path_east, path_north, w_embed, root_rows)
    projected = jnp.einsum(
        "cfd,hjdk->cfhjk", normed_e.astype(jnp.bfloat16), w_all, preferred_element_type=jnp.float32
    )
    query_unit, query_len = unit_rows(projected[:, :, :, 0])
    key_unit, key_len = unit_rows(projected[:, :, :, 1])
    asking_vectors_group = query_unit.astype(jnp.bfloat16)
    lookup_vectors_group = key_unit.astype(jnp.bfloat16)
    value_b = projected[:, :, :, 2].astype(jnp.bfloat16)
    similarity_table = normalizing_sharpness * jnp.einsum(
        "cfhd,cghd->chfg",
        asking_vectors_group,
        lookup_vectors_group,
        preferred_element_type=jnp.float32,
    )
    expo = jnp.exp(similarity_table)
    focus_probabilities = expo / jnp.sum(expo, axis=-1, keepdims=True)
    attention_b = focus_probabilities.astype(jnp.bfloat16)
    column_mass = jnp.sum(attention_b, axis=2, dtype=jnp.float32)
    value_f = value_b.astype(jnp.float32)
    pooled = jnp.einsum("chg,cghd->chd", column_mass, value_f, precision=highest)
    pooled_b = pooled.astype(jnp.bfloat16).reshape(clips_dev, D_REW)
    motion_emb = jnp.dot(
        pooled_b, proj_rows.astype(jnp.bfloat16), preferred_element_type=jnp.float32
    )
    prompts = lax.dynamic_slice_in_dim(prompt_index, me * clips_dev, clips_dev)
    weights = lax.dynamic_slice_in_dim(reward_weight, me * clips_dev, clips_dev)
    choose = (prompts[:, None] == jnp.arange(PROMPTS)[None, :]).astype(jnp.float32)
    target = jnp.dot(choose, text_unit, precision=highest)
    emb_len = jnp.sqrt(jnp.sum(motion_emb * motion_emb, axis=-1) + epsilon)
    rewards = jnp.sum(motion_emb * target, axis=-1) / emb_len
    d_memb = (
        (-weights)[:, None]
        * (target - rewards[:, None] * motion_emb / emb_len[:, None])
        / emb_len[:, None]
    )
    d_pooled = jnp.dot(d_memb, proj_rows.T, precision=highest).reshape(clips_dev, HEADS, head_size)
    reduction_dimension = jnp.einsum("chd,cghd->chg", d_pooled, value_f, precision=highest)
    d_value = jnp.transpose(column_mass, (0, 2, 1))[..., None] * d_pooled[:, None]
    pairwise_dot_similarity = jnp.sum(
        focus_probabilities * reduction_dimension[:, :, None, :], axis=-1, keepdims=True
    )
    similarity_derivative = (
        normalizing_sharpness
        * focus_probabilities
        * (reduction_dimension[:, :, None, :] - pairwise_dot_similarity)
    ).astype(jnp.bfloat16)
    d_qu = jnp.einsum(
        "chfg,cghd->cfhd",
        similarity_derivative,
        lookup_vectors_group,
        preferred_element_type=jnp.float32,
    )
    d_ku = jnp.einsum(
        "chfg,cfhd->cghd",
        similarity_derivative,
        asking_vectors_group,
        preferred_element_type=jnp.float32,
    )
    d_query = (d_qu - query_unit * jnp.sum(query_unit * d_qu, axis=-1, keepdims=True)) / query_len
    d_key = (d_ku - key_unit * jnp.sum(key_unit * d_ku, axis=-1, keepdims=True)) / key_len
    d_proj = jnp.stack([d_query, d_key, d_value], axis=3).astype(jnp.bfloat16)
    d_emb = jnp.einsum("cfhjk,hjdk->cfd", d_proj, w_all, preferred_element_type=jnp.float32)
    d_motion = motion_grad(d_emb, normed_e, scale_rms, x_clean, theta, embed_rows, root_rows)
    d_eps_b = (-level * d_motion).astype(jnp.bfloat16)
    d_mod = jnp.einsum("cfe,de->cfd", d_eps_b, w_out, preferred_element_type=jnp.float32)
    d_norm = d_mod * gain
    grad_hidden = (
        inv_std
        * (
            d_norm
            - jnp.mean(d_norm, axis=-1, keepdims=True)
            - normed_h * jnp.mean(d_norm * normed_h, axis=-1, keepdims=True)
        )
    ).astype(jnp.bfloat16)
    grad_term = jnp.einsum("cfd,cfe->de", modulated, d_eps_b, preferred_element_type=jnp.float32)
    rows_dev = w_out.shape[0] // ways
    cols = grad_term.shape[1]
    n_dp = lax.axis_size("dp")
    total_clips = clips_dev * ways * n_dp * lax.axis_size("sec")
    extra = -(-total_clips // cols)
    extra = -(-extra // 8) * 8
    first_clip = ((lax.axis_index("sec") * n_dp + lax.axis_index("dp")) * ways + me) * clips_dev
    columns = jnp.arange(extra * cols)
    slots = columns[None, :] == (first_clip + jnp.arange(clips_dev))[:, None]
    reward_rows = jnp.sum(jnp.where(slots, rewards[:, None], 0.0), axis=0).reshape(extra, cols)
    stacked = jnp.concatenate(
        [
            grad_term.reshape(ways, rows_dev, cols),
            jnp.broadcast_to(reward_rows[None], (ways, extra, cols)),
        ],
        axis=1,
    ).reshape(ways * (rows_dev + extra), cols)
    block = lax.psum_scatter(stacked, "seq", scatter_dimension=0, tiled=True)
    block = lax.psum(block, ("sec", "dp"))
    grad_w_out = block[:rows_dev]
    group_first = (lax.axis_index("sec") * n_dp + lax.axis_index("dp")) * ways * clips_dev
    all_rewards = block[rows_dev:].reshape(extra * cols)
    rewards_out = lax.dynamic_slice_in_dim(all_rewards, group_first, ways * clips_dev)
    return (rewards_out, grad_w_out, grad_hidden)


def solution(mesh):
    placed = (
        P(("sec", "dp", "seq"), None, None),
        P(("sec", "dp", "seq"), None),
        P(("sec", "dp", "seq"), None),
        P(("sec", "dp", "seq"), None, None),
        P(("sec", "dp", "seq")),
        P(),
        P(),
        P(),
        P(None, None, "seq"),
        P("seq", None),
        P("seq", None),
        P(),
        P(("sec", "dp")),
        P(("sec", "dp")),
    )
    return jax.shard_map(
        local,
        mesh=mesh,
        in_specs=placed,
        out_specs=(P(("sec", "dp")), P("seq", None), P(("sec", "dp", "seq"), None, None)),
        check_vma=False,
    )
```

profile of v0, /device:TPU:32, one launch (start us, length us, event | category | flops | bytes accessed | tf_op | source)
XLA Modules:
  0.0 444.6 jit_solution(8635623600535376236)
XLA Ops:
  9.1 5.1 %gather_fusion = bf16[1024,512]{1,0:T(8,128)(2,1)} fusion(bf16[3088,512]{1,0:T(8,128)(2,1)S(1)} %copy-done, s32[1024]{0:T(1024)S(1)} %broadcast_clamp_fusion), kind=kCustom, calls=%fused_computation | custom fusion | bytes 2101248 | tf_op jit(solution)/shard_map/jit(_take)/gather | solution.py:93
  14.2 1.6 select_reduce_fusion
  20.1 1.3 convert_reduce_fusion
  21.4 1.4 fusion.19
  22.8 2.0 fusion.21
  30.1 2.7 multiply_reduce_fusion.4
  32.8 29.8 %all-gather.7.cloned.1.call-done = f32[2560,512]{1,0:T(8,128)} async-done(((f32[160,512]{1,0:T(8,128)}), f32[2560,512]{1,0:T(8,128)}) %all-gather.7.cloned.1.call-update) | async-done | bytes 5242896 | tf_op jit(solution)/shard_map/all_gather | solution.py:98
  62.6 1.3 slice_reduce_fusion
  64.9 131.2 %all-gather.5.cloned.1.call-done = bf16[48,2048,128]{2,1,0:T(8,128)(2,1)} async-done(((bf16[3,2048,128]{2,1,0:T(8,128)(2,1)}), bf16[48,2048,128]{2,1,0:T(8,128)(2,1)}) %all-gather.5.cloned.1.call-update) | async-done | bytes 25165840 | tf_op jit(solution)/shard_map/all_gather | solution.py:104
  196.1 16.0 %convolution_bitcast_fusion.1 = f32[1,128,16,3,128]{1,4,3,2,0:T(8,128)} fusion(bf16[16,3,2048,128]{3,2,1,0:T(8,128)(2,1)} %bitcast.182, f32[128,2048]{1,0:T(8,128)} %get-tuple-element.74, f32[128]{0:T(128)S(1)} %add_sqrt_fusion.3), kind=kOutput, calls=%fused_computation.12 | convolution fusion | flops 3221749760 | bytes 29360640 | tf_op jit(solution)/shard_map/cfd,hjdk->cfhjk/dot_general | solution.py:116
  212.2 1.7 fusion.22
  213.9 2.8 fusion.23
  216.7 2.7 convert_reduce_fusion.1
  219.4 2.1 fusion.34
  221.5 2.6 fusion.4
  226.1 5.4 %fusion.1 = f32[1,16,128]{2,0,1:T(1,128)S(1)} fusion(f32[512,1,1]{0,1,2:T(1,128)S(1)} %bitcast.203, f32[16,160,512]{2,1,0:T(8,128)} %bitcast.186), kind=kOutput, calls=%fused_computation.2 | convolution fusion | flops 12582912 | bytes 4204544 | tf_op jit(solution)/shard_map/dot_general | solution.py:151
  234.9 1.1 multiply_convert_fusion
  236.1 1.6 fusion.30
  237.6 14.5 %multiply_reduce_fusion = (f32[128]{0:T(128)S(1)}, f32[128,2048]{1,0:T(8,128)}) fusion(f32[128,2048]{1,0:T(8,128)} %get-tuple-element.74, f32[128]{0:T(128)S(1)} %add_sqrt_fusion.3, bf16[16,3,2048,128]{3,2,1,0:T(8,128)(2,1)} %bitcast.183, bf16[128,16,1,128]{0,3,1,2:T(8,128)(2,1)} %multiply_convert_fusion, bf16[128,16,1,128]{0,3,1,2:T(8,128)(2,1)} %get-tuple-element.60, ...), kind=kOutput, calls=%fused_computation.50 | convolution fusion | flops 3223584768 | bytes 28836864 | tf_op jit(solution)/shard_map/cfhjk,hjdk->cfd/dot_general | solution.py:177
  252.2 3.7 multiply_reduce_fusion.8
  256.5 1.9 fusion.56
  258.8 2.7 fusion.66
  261.5 1.3 fusion.36
  265.2 3.2 fusion.15
  268.4 1.5 reduce_sum.241
  269.9 3.1 fusion.18
  273.0 2.2 copy.68
  275.2 1.6 fusion.37
  276.8 1.8 pad_maximum_fusion
  278.7 57.8 %reduce-scatter.2.cloned.1.call-done = f32[168,256]{1,0:T(8,128)} async-done(((f32[2688,256]{1,0:T(8,128)}), f32[168,256]{1,0:T(8,128)}) %reduce-scatter.2.cloned.1.call-update) | async-done | bytes 172048 | tf_op jit(solution)/shard_map/reduce_scatter | solution.py:208
  336.6 98.6 %all-reduce.2.cloned.1.call-done = f32[168,256]{1,0:T(8,128)} async-done(((f32[168,256]{1,0:T(8,128)}), f32[168,256]{1,0:T(8,128)}) %all-reduce.2.cloned.1.call-update) | async-done | bytes 172048 | tf_op jit(solution)/shard_map/psum | solution.py:209
  436.5 1.6 slice.138
  (122 shorter events, 19.9 us)
Async XLA Ops:
  7.2 2.0 copy-start
  7.2 55.4 %all-gather.7.cloned.1.call-start = ((), (), s32[]{:S(2)}) async-start(), calls=%async_computation.4 | async-start | bytes 5570560 | tf_op jit(solution)/shard_map/all_gather | solution.py:98
  15.8 2.3 copy-start.29
  15.9 3.5 copy-start.30
  15.9 4.1 copy-start.16
  15.9 4.1 copy-start.17
  16.6 6.2 %copy-start.28 = (bf16[1,128,256]{2,1,0:T(8,128)(2,1)S(1)}, bf16[1,128,256]{2,1,0:T(8,128)(2,1)}, u32[]{:S(2)}) copy-start(bf16[1,128,256]{2,1,0:T(8,128)(2,1)} %param.23) | copy-start | bytes 196612
  16.7 179.5 %all-gather.5.cloned.1.call-start = ((), (), s32[]{:S(2)}) async-start(), calls=%async_computation.3 | async-start | bytes 26738688 | tf_op jit(solution)/shard_map/all_gather | solution.py:104
  17.4 319.1 %reduce-scatter.2.cloned.1.call-start = ((), (), s32[]{:S(2)}) async-start(), calls=%async_computation.1 | async-start | bytes 2924544 | tf_op jit(solution)/shard_map/reduce_scatter | solution.py:208
  20.1 4.7 %copy-start.7 = (f32[2560]{0:T(1024)}, f32[2560]{0:T(1024)S(1)}, u32[]{:S(2)}) copy-start(f32[2560]{0:T(1024)S(1)} %get-tuple-element.83) | copy-start | bytes 30724
  20.1 4.7 %copy-start.9 = (f32[2560]{0:T(1024)}, f32[2560]{0:T(1024)S(1)}, u32[]{:S(2)}) copy-start(f32[2560]{0:T(1024)S(1)} %get-tuple-element.82) | copy-start | bytes 30724
  21.4 3.4 copy-start.18
  22.8 2.8 copy-start.26
  27.3 36.6 %copy-start.4 = (f32[1,128,1]{2,1,0:T(8,128)}, f32[1,128,1]{2,1,0:T(8,128)S(1)}, u32[]{:S(2)}) copy-start(f32[1,128,1]{2,1,0:T(8,128)S(1)} %get-tuple-element.66) | copy-start | bytes 1540
  30.1 32.5 %copy-start.11 = (f32[1,2048]{1,0:T(1,128)}, f32[1,2048]{1,0:T(1,128)S(1)}, u32[]{:S(2)}) copy-start(f32[1,2048]{1,0:T(1,128)S(1)} %get-tuple-element.68) | copy-start | bytes 24580
  30.1 32.5 %copy-start.13 = (f32[1,2048]{1,0:T(1,128)}, f32[1,2048]{1,0:T(1,128)S(1)}, u32[]{:S(2)}) copy-start(f32[1,2048]{1,0:T(1,128)S(1)} %get-tuple-element.69) | copy-start | bytes 24580
  226.1 6.1 %copy-start.1 = (f32[1,128,16,3,128]{1,4,3,2,0:T(8,128)S(1)}, f32[1,128,16,3,128]{1,4,3,2,0:T(8,128)}, u32[]{:S(2)}) copy-start(f32[1,128,16,3,128]{1,4,3,2,0:T(8,128)} %convolution_bitcast_fusion.1) | copy-start | bytes 9437188
  231.5 1.2 copy-start.2
  231.5 1.6 copy-start.3
  237.6 14.5 %copy-start.12 = (f32[1,2048]{1,0:T(1,128)S(1)}, f32[1,2048]{1,0:T(1,128)}, u32[]{:S(2)}) copy-start(f32[1,2048]{1,0:T(1,128)} %copy-done.11) | copy-start | bytes 24580
  237.6 14.5 %copy-start.14 = (f32[1,2048]{1,0:T(1,128)S(1)}, f32[1,2048]{1,0:T(1,128)}, u32[]{:S(2)}) copy-start(f32[1,2048]{1,0:T(1,128)} %copy-done.13) | copy-start | bytes 24580
  252.1 4.3 copy-start.20
  252.1 4.3 copy-start.21
  252.1 4.3 copy-start.23
  252.1 4.3 copy-start.25
  252.1 6.5 %copy-start.5 = (f32[1,128,1]{2,1,0:T(8,128)S(1)}, f32[1,128,1]{2,1,0:T(8,128)}, u32[]{:S(2)}) copy-start(f32[1,128,1]{2,1,0:T(8,128)} %copy-done.4) | copy-start | bytes 1540
  265.1 4.7 %copy-start.8 = (f32[2560]{0:T(1024)S(1)}, f32[2560]{0:T(1024)}, u32[]{:S(2)}) copy-start(f32[2560]{0:T(1024)} %copy-done.7) | copy-start | bytes 30724
  265.2 4.7 %copy-start.10 = (f32[2560]{0:T(1024)S(1)}, f32[2560]{0:T(1024)}, u32[]{:S(2)}) copy-start(f32[2560]{0:T(1024)} %copy-done.9) | copy-start | bytes 30724
  265.2 4.7 %copy-start.19 = (f32[128]{0:T(128)S(1)}, f32[128]{0:T(128)}, u32[]{:S(2)}) copy-start(f32[128]{0:T(128)} %copy-done.18) | copy-start | bytes 1540
  265.2 4.7 %copy-start.27 = (f32[128]{0:T(128)S(1)}, f32[128]{0:T(128)}, u32[]{:S(2)}) copy-start(f32[128]{0:T(128)} %copy-done.26) | copy-start | bytes 1540
  275.2 1.6 copy-start.15
  278.6 156.6 %all-reduce.2.cloned.1.call-start = ((), (), s32[]{:S(2)}) async-start(), calls=%async_computation.2 | async-start | bytes 344064 | tf_op jit(solution)/shard_map/psum | solution.py:209
  (3 other events, 2.2 us)
Sparse Core Ops, SparseCore 0:
  16.8 45.7 all-gather.6
  64.4 131.6 all-gather.4
  278.8 57.7 reduce-scatter.1
  340.0 95.2 all-reduce.1
where the time goes:
time: 446 us; the launch traced here: 445 us
  waiting for transfers between devices  318 us (71%)
  matrix products  58.1 us (13%)
  other arithmetic  34.6 us (8%)
  between operations  16.9 us (4%)
  local copies, waits for them, and re-layouts  16.6 us (4%)
    all_gather x1, waiting for transfers between devices, local(): w_all = lax.all_gather(w_qkv, 'seq', axis=0)  131 us
    psum x1, waiting for transfers between devices, local(): block = lax.psum(block, ('sec', 'dp'))  98.6 us
    reduce_scatter x1, waiting for transfers between devices, local(): block = lax.psum_scatter(stacked, 'seq', scatter_dimension=0, tiled=True)  57.8 us
    all_gather x1, waiting for transfers between devices, local(): lax.all_gather(jnp.concatenate([w_proj.astype(jnp.float32), text_part], a...  29.8 us
    dot_general x1, matrix products, local(): jnp.einsum('cfd,hjdk->cfhjk', normed_e.astype(jnp.bfloat16), w_all, prefe...  16 us
    dot_general x1, matrix products, local(): jnp.einsum('cfhjk,hjdk->cfd', d_proj, w_all, preferred_element_type=jnp.f...  14.5 us
  transfers between devices with their start and end apart: 4, of which 4 were waited for; matrix products, arithmetic and copies ran while one was open for 3% of the time, Pallas kernels for 0%

commit v1 on v0

--- a/solution.py
+++ b/solution.py
@@ -206,7 +206,7 @@
         axis=1,
     ).reshape(ways * (rows_dev + extra), cols)
     block = lax.psum_scatter(stacked, "seq", scatter_dimension=0, tiled=True)
-    block = lax.psum(block, ("sec", "dp"))
+    block = lax.psum(lax.psum(block, "sec"), "dp")
     grad_w_out = block[:rows_dev]
     group_first = (lax.axis_index("sec") * n_dp + lax.axis_index("dp")) * ways * clips_dev
     all_rewards = block[rows_dev:].reshape(extra * cols)

time: 446 us -> 477 us (1.070)
  waiting for transfers between devices: 318 us -> 349 us
    psum x1 -> x2, waiting for transfers between devices: 98.6 us -> 130 us  [local(): block = lax.psum(lax.psum(block, 'sec'), 'dp')]
  transfers between devices with their start and end apart: 4 -> 5, of which waited for: 4 -> 5; matrix products, arithmetic and copies ran while one was open for 3% -> 3% of each run, Pallas kernels for 0% -> 0%
where the time goes in v1:
time: 477 us; the launch traced here: 476 us
  waiting for transfers between devices  349 us (73%)
  matrix products  58.1 us (12%)
  other arithmetic  34.6 us (7%)
  between operations  16.9 us (4%)
  local copies, waits for them, and re-layouts  16.6 us (3%)
    all_gather x1, waiting for transfers between devices, local(): w_all = lax.all_gather(w_qkv, 'seq', axis=0)  131 us
    psum x2, waiting for transfers between devices, local(): block = lax.psum(lax.psum(block, 'sec'), 'dp')  130 us
    reduce_scatter x1, waiting for transfers between devices, local(): block = lax.psum_scatter(stacked, 'seq', scatter_dimension=0, tiled=True)  57.8 us
    all_gather x1, waiting for transfers between devices, local(): lax.all_gather(jnp.concatenate([w_proj.astype(jnp.float32), text_part], a...  29.8 us
    dot_general x1, matrix products, local(): jnp.einsum('cfd,hjdk->cfhjk', normed_e.astype(jnp.bfloat16), w_all, prefe...  16 us
    dot_general x1, matrix products, local(): jnp.einsum('cfhjk,hjdk->cfd', d_proj, w_all, preferred_element_type=jnp.f...  14.5 us
  transfers between devices with their start and end apart: 5, of which 5 were waited for; matrix products, arithmetic and copies ran while one was open for 3% of the time, Pallas kernels for 0%

profile of v1, /device:TPU:32, one launch (start us, length us, event | category | flops | bytes accessed | tf_op | source)
XLA Modules:
  0.0 475.8 jit_solution(4514642923485365420)
XLA Ops:
  9.1 5.1 %gather_fusion = bf16[1024,512]{1,0:T(8,128)(2,1)} fusion(bf16[3088,512]{1,0:T(8,128)(2,1)S(1)} %copy-done, s32[1024]{0:T(1024)S(1)} %broadcast_clamp_fusion), kind=kCustom, calls=%fused_computation | custom fusion | bytes 2101248 | tf_op jit(solution)/shard_map/jit(_take)/gather | solution.py:93
  14.2 1.6 select_reduce_fusion
  20.1 1.3 convert_reduce_fusion
  21.4 1.4 fusion.19
  22.8 2.0 fusion.21
  30.1 2.7 multiply_reduce_fusion.4
  32.8 29.8 %all-gather.7.cloned.1.call-done = f32[2560,512]{1,0:T(8,128)} async-done(((f32[160,512]{1,0:T(8,128)}), f32[2560,512]{1,0:T(8,128)}) %all-gather.7.cloned.1.call-update) | async-done | bytes 5242896 | tf_op jit(solution)/shard_map/all_gather | solution.py:98
  62.6 1.3 slice_reduce_fusion
  64.9 131.2 %all-gather.5.cloned.1.call-done = bf16[48,2048,128]{2,1,0:T(8,128)(2,1)} async-done(((bf16[3,2048,128]{2,1,0:T(8,128)(2,1)}), bf16[48,2048,128]{2,1,0:T(8,128)(2,1)}) %all-gather.5.cloned.1.call-update) | async-done | bytes 25165840 | tf_op jit(solution)/shard_map/all_gather | solution.py:104
  196.1 16.0 %convolution_bitcast_fusion.1 = f32[1,128,16,3,128]{1,4,3,2,0:T(8,128)} fusion(bf16[16,3,2048,128]{3,2,1,0:T(8,128)(2,1)} %bitcast.182, f32[128,2048]{1,0:T(8,128)} %get-tuple-element.74, f32[128]{0:T(128)S(1)} %add_sqrt_fusion.3), kind=kOutput, calls=%fused_computation.12 | convolution fusion | flops 3221749760 | bytes 29360640 | tf_op jit(solution)/shard_map/cfd,hjdk->cfhjk/dot_general | solution.py:116
  212.2 1.7 fusion.22
  213.9 2.8 fusion.23
  216.7 2.7 convert_reduce_fusion.1
  219.4 2.1 fusion.34
  221.5 2.6 fusion.4
  226.1 5.4 %fusion.1 = f32[1,16,128]{2,0,1:T(1,128)S(1)} fusion(f32[512,1,1]{0,1,2:T(1,128)S(1)} %bitcast.203, f32[16,160,512]{2,1,0:T(8,128)} %bitcast.186), kind=kOutput, calls=%fused_computation.2 | convolution fusion | flops 12582912 | bytes 4204544 | tf_op jit(solution)/shard_map/dot_general | solution.py:151
  236.1 1.6 fusion.30
  237.6 14.5 %multiply_reduce_fusion = (f32[128]{0:T(128)S(1)}, f32[128,2048]{1,0:T(8,128)}) fusion(f32[128,2048]{1,0:T(8,128)} %get-tuple-element.74, f32[128]{0:T(128)S(1)} %add_sqrt_fusion.3, bf16[16,3,2048,128]{3,2,1,0:T(8,128)(2,1)} %bitcast.183, bf16[128,16,1,128]{0,3,1,2:T(8,128)(2,1)} %multiply_convert_fusion, bf16[128,16,1,128]{0,3,1,2:T(8,128)(2,1)} %get-tuple-element.60, ...), kind=kOutput, calls=%fused_computation.50 | convolution fusion | flops 3223584768 | bytes 28836864 | tf_op jit(solution)/shard_map/cfhjk,hjdk->cfd/dot_general | solution.py:177
  252.2 3.7 multiply_reduce_fusion.8
  256.5 1.9 fusion.56
  258.8 2.7 fusion.66
  261.5 1.3 fusion.36
  265.2 3.2 fusion.15
  268.4 1.5 reduce_sum.241
  269.9 3.1 fusion.18
  273.0 2.2 copy.68
  275.2 1.6 fusion.37
  276.8 1.8 pad_maximum_fusion
  278.7 57.8 %reduce-scatter.2.cloned.1.call-done = f32[168,256]{1,0:T(8,128)} async-done(((f32[2688,256]{1,0:T(8,128)}), f32[168,256]{1,0:T(8,128)}) %reduce-scatter.2.cloned.1.call-update) | async-done | bytes 172048 | tf_op jit(solution)/shard_map/reduce_scatter | solution.py:208
  336.6 38.0 %all-reduce.3.cloned.1.call-done = f32[168,256]{1,0:T(8,128)} async-done(((f32[168,256]{1,0:T(8,128)}), f32[168,256]{1,0:T(8,128)}) %all-reduce.3.cloned.1.call-update) | async-done | bytes 172048 | tf_op jit(solution)/shard_map/psum | solution.py:209
  374.6 91.7 %all-reduce.5.cloned.1.call-done = f32[168,256]{1,0:T(8,128)} async-done(((f32[168,256]{1,0:T(8,128)}), f32[168,256]{1,0:T(8,128)}) %all-reduce.5.cloned.1.call-update) | async-done | bytes 172048 | tf_op jit(solution)/shard_map/psum | solution.py:209
  467.7 1.6 slice.138
  (125 shorter events, 21.1 us)
Async XLA Ops:
  7.2 2.0 copy-start
  7.2 55.4 %all-gather.7.cloned.1.call-start = ((), (), s32[]{:S(2)}) async-start(), calls=%async_computation.5 | async-start | bytes 5570560 | tf_op jit(solution)/shard_map/all_gather | solution.py:98
  15.8 2.3 copy-start.29
  15.9 3.5 copy-start.30
  15.9 4.1 copy-start.16
  15.9 4.1 copy-start.17
  16.6 6.2 %copy-start.28 = (bf16[1,128,256]{2,1,0:T(8,128)(2,1)S(1)}, bf16[1,128,256]{2,1,0:T(8,128)(2,1)}, u32[]{:S(2)}) copy-start(bf16[1,128,256]{2,1,0:T(8,128)(2,1)} %param.23) | copy-start | bytes 196612
  16.7 179.5 %all-gather.5.cloned.1.call-start = ((), (), s32[]{:S(2)}) async-start(), calls=%async_computation.4 | async-start | bytes 26738688 | tf_op jit(solution)/shard_map/all_gather | solution.py:104
  17.4 319.1 %reduce-scatter.2.cloned.1.call-start = ((), (), s32[]{:S(2)}) async-start(), calls=%async_computation.1 | async-start | bytes 2924544 | tf_op jit(solution)/shard_map/reduce_scatter | solution.py:208
  20.1 4.7 copy-start.7
  20.1 4.7 copy-start.9
  21.4 3.4 copy-start.18
  22.8 2.8 copy-start.26
  27.3 36.6 %copy-start.4 = (f32[1,128,1]{2,1,0:T(8,128)}, f32[1,128,1]{2,1,0:T(8,128)S(1)}, u32[]{:S(2)}) copy-start(f32[1,128,1]{2,1,0:T(8,128)S(1)} %get-tuple-element.66) | copy-start | bytes 1540
  30.1 32.5 %copy-start.11 = (f32[1,2048]{1,0:T(1,128)}, f32[1,2048]{1,0:T(1,128)S(1)}, u32[]{:S(2)}) copy-start(f32[1,2048]{1,0:T(1,128)S(1)} %get-tuple-element.68) | copy-start | bytes 24580
  30.1 32.5 %copy-start.13 = (f32[1,2048]{1,0:T(1,128)}, f32[1,2048]{1,0:T(1,128)S(1)}, u32[]{:S(2)}) copy-start(f32[1,2048]{1,0:T(1,128)S(1)} %get-tuple-element.69) | copy-start | bytes 24580
  226.1 6.1 %copy-start.1 = (f32[1,128,16,3,128]{1,4,3,2,0:T(8,128)S(1)}, f32[1,128,16,3,128]{1,4,3,2,0:T(8,128)}, u32[]{:S(2)}) copy-start(f32[1,128,16,3,128]{1,4,3,2,0:T(8,128)} %convolution_bitcast_fusion.1) | copy-start | bytes 9437188
  231.5 1.6 copy-start.3
  237.6 14.5 %copy-start.12 = (f32[1,2048]{1,0:T(1,128)S(1)}, f32[1,2048]{1,0:T(1,128)}, u32[]{:S(2)}) copy-start(f32[1,2048]{1,0:T(1,128)} %copy-done.11) | copy-start | bytes 24580
  237.6 14.5 %copy-start.14 = (f32[1,2048]{1,0:T(1,128)S(1)}, f32[1,2048]{1,0:T(1,128)}, u32[]{:S(2)}) copy-start(f32[1,2048]{1,0:T(1,128)} %copy-done.13) | copy-start | bytes 24580
  252.1 4.3 copy-start.20
  252.1 4.3 copy-start.21
  252.1 4.3 copy-start.23
  252.1 4.3 copy-start.25
  252.1 6.5 %copy-start.5 = (f32[1,128,1]{2,1,0:T(8,128)S(1)}, f32[1,128,1]{2,1,0:T(8,128)}, u32[]{:S(2)}) copy-start(f32[1,128,1]{2,1,0:T(8,128)} %copy-done.4) | copy-start | bytes 1540
  265.1 4.7 copy-start.8
  265.2 4.7 copy-start.10
  265.2 4.7 copy-start.19
  265.2 4.7 copy-start.27
  275.2 1.6 copy-start.15
  278.6 96.0 %all-reduce.3.cloned.1.call-start = ((), (), s32[]{:S(2)}) async-start(), calls=%async_computation.2 | async-start | bytes 344064 | tf_op jit(solution)/shard_map/psum | solution.py:209
  336.6 129.8 %all-reduce.5.cloned.1.call-start = ((), (), s32[]{:S(2)}) async-start(), calls=%async_computation.3 | async-start | bytes 344064 | tf_op jit(solution)/shard_map/psum | solution.py:209
  (4 other events, 3.4 us)
Sparse Core Ops, SparseCore 0:
  16.8 45.7 all-gather.6
  64.4 131.6 all-gather.4
  278.8 57.7 reduce-scatter.1
  339.1 35.4 all-reduce.2
  377.3 89.0 all-reduce.4
